TPU v7x, 32 devices: a whole 2x2x4 slice. The times are simulated.
32 devices in a mesh: seq: 8 (over y, x, core), tp: 4 (over z).
Axes of the slice: x: 2, y: 2, z: 4, core: 2. Of those that a mesh axis runs over, the one named last changes fastest.
Arguments:
- projected: bfloat16 [1536, 3, 8192], P('seq', None, 'tp'), may hold values from -6 to 6
- feat_taps: float32 [7, 3, 8192], P(None, None, 'tp'), may hold values from -2.5 to 2.5
- filters: float32 [512, 128], P('tp'), may hold values from -1.5 to 1.5
- out_weight: bfloat16 [8192, 8192], P('tp'), may hold values from -0.09375 to 0.09375
- cotangent: bfloat16 [1536, 8192], P('seq', 'tp'), may hold values from -6 to 6
Outputs:
- output: bfloat16 [1536, 8192], P('seq', 'tp')
- input_grad: bfloat16 [1536, 3, 8192], P('seq', None, 'tp')
All inputs are finite; a program needn't handle non-finite values.
Results may differ from a plain program's by a relative error of at most 0.0095.
Values may be sent and summed in bfloat16 or wider, within the bound.
No kernel may reach another device: no remote copies, remote signals or barrier semaphores. Data moves between devices by JAX's collectives and lax.ppermute only.
A program may use at most 128 MiB of HBM per device.

v0:
```python
import jax
import jax.numpy as jnp
from jax import lax
from jax.experimental import pallas as pl
from jax.experimental.pallas import tpu as pltpu
from jax.sharding import PartitionSpec as P

LANES = 128


def _toeplitz_kernel(base_ref, ext_ref, out_ref):
    gb, span = base_ref.shape
    rows, width = out_ref.shape
    hg = width // gb
    p = ext_ref[...]
    p_hi = p.astype(jnp.bfloat16)
    p_lo = (p - p_hi.astype(jnp.float32)).astype(jnp.bfloat16)
    lane_group = lax.broadcasted_iota(jnp.int32, (span, width), 1) // hg
    zero = jnp.zeros_like(p_hi)
    acc = jnp.zeros((rows, width), jnp.float32)
    for g in range(gb):
        t = jnp.broadcast_to(base_ref[pl.ds(g, 1), :], (rows, span))
        t = pltpu.roll(t, 0, 1, stride=1, stride_axis=0)
        t_hi = t.astype(jnp.bfloat16)
        t_lo = (t - t_hi.astype(jnp.float32)).astype(jnp.bfloat16)
        m = lane_group == g
        ph = jnp.where(m, p_hi, zero)
        plo = jnp.where(m, p_lo, zero)
        acc = acc + jnp.dot(t_hi, ph, preferred_element_type=jnp.float32)
        acc = acc + jnp.dot(t_hi, plo, preferred_element_type=jnp.float32)
        acc = acc + jnp.dot(t_lo, ph, preferred_element_type=jnp.float32)
    out_ref[...] = acc


def toeplitz_conv(base, ext, rows):
    groups, span = base.shape
    channels = ext.shape[1]
    gb = groups * LANES // channels
    steps = channels // LANES
    flops = 6 * rows * span * LANES * gb * steps
    return pl.pallas_call(
        _toeplitz_kernel,
        grid=(steps,),
        in_specs=[
            pl.BlockSpec((gb, span), lambda i: (i, 0)),
            pl.BlockSpec((span, LANES), lambda i: (0, i)),
        ],
        out_specs=pl.BlockSpec((rows, LANES), lambda i: (0, i)),
        out_shape=jax.ShapeDtypeStruct((rows, channels), jnp.float32),
        cost_estimate=pl.CostEstimate(
            flops=flops, transcendentals=0,
            bytes_accessed=4 * (base.size + ext.size + rows * channels)),
    )(base, ext)


def shift_perm(n, step):
    if step > 0:
        return [(j, j + 1) for j in range(n - 1)]
    return [(j + 1, j) for j in range(n - 1)]


def body(projected, feat_taps, filters, out_weight, cotangent):
    rows = projected.shape[0]
    feat_len = feat_taps.shape[0]
    filt_len = filters.shape[1]
    channels = projected.shape[2]
    n = lax.axis_size("seq")
    fwd = shift_perm(n, 1)
    bwd = shift_perm(n, -1)
    fh = feat_len - 1
    lh = filt_len - 1
    assert fh <= rows and lh <= rows

    span = -(-(rows + lh) // LANES) * LANES
    tail = span - filt_len
    base_fwd = jnp.pad(filters[:, ::-1], ((0, 0), (0, tail)))
    base_bwd = jnp.pad(filters, ((0, 0), (0, tail)))

    prev_proj = lax.ppermute(projected[rows - fh:], "seq", fwd)
    ext = jnp.concatenate([prev_proj, projected], axis=0).astype(jnp.float32)
    feats = feat_taps[0] * ext[fh:fh + rows]
    for d in range(1, feat_len):
        feats = feats + feat_taps[d] * ext[fh - d:fh - d + rows]
    query = feats[:, 0]
    key_feat = feats[:, 1]
    value_feat = feats[:, 2]
    product = key_feat * value_feat

    prev_prod = lax.ppermute(product[rows - lh:], "seq", fwd)
    pext = jnp.concatenate(
        [prev_prod, product, jnp.zeros((span - rows - lh, channels), jnp.float32)], axis=0
    )
    conv = toeplitz_conv(base_fwd, pext, rows)
    mixed = (query * conv).astype(jnp.bfloat16)

    partial = jnp.einsum(
        "tc,cd->td", mixed, out_weight, preferred_element_type=jnp.float32
    ).astype(jnp.bfloat16)
    output = lax.psum_scatter(partial, "tp", scatter_dimension=1, tiled=True)

    cot_full = lax.all_gather(cotangent, "tp", axis=1, tiled=True)
    grad_mixed = jnp.einsum(
        "te,ce->tc", cot_full, out_weight, preferred_element_type=jnp.float32
    )
    signal_grad = grad_mixed * query
    query_grad = grad_mixed * conv
    next_sig = lax.ppermute(signal_grad[:lh], "seq", bwd)
    sext = jnp.concatenate(
        [signal_grad, next_sig, jnp.zeros((span - rows - lh, channels), jnp.float32)], axis=0
    )
    conv_grad = toeplitz_conv(base_bwd, sext, rows)
    dfeat = jnp.stack([query_grad, conv_grad * value_feat, conv_grad * key_feat], axis=1)
    next_dfeat = lax.ppermute(dfeat[:fh], "seq", bwd)
    dext = jnp.concatenate([dfeat, next_dfeat], axis=0)
    igrad = feat_taps[0] * dext[:rows]
    for d in range(1, feat_len):
        igrad = igrad + feat_taps[d] * dext[d:d + rows]
    return output, igrad.astype(jnp.bfloat16)


def solution(mesh):
    in_specs = (
        P("seq", None, "tp"),
        P(None, None, "tp"),
        P("tp", None),
        P("tp", None),
        P("seq", "tp"),
    )
    out_specs = (P("seq", "tp"), P("seq", None, "tp"))
    return jax.shard_map(body, mesh=mesh, in_specs=in_specs, out_specs=out_specs, check_vma=False)
```

profile of v0, /device:TPU:0, one launch (start us, length us, event | category | flops | bytes accessed | tf_op | source)
XLA Modules:
  0.0 259.9 jit_solution(6661388206705830584)
XLA Ops:
  7.2 0.7 all-gather.2.cloned.1.call-update
  7.9 0.9 slice.89
  8.9 2.4 collective-permute-start
  11.3 1.8 fusion.15
  13.3 2.4 maximum_convert_fusion
  15.7 5.3 %fusion.7 = f32[192,3,2048]{2,0,1:T(8,128)} fusion(f32[198,3,2048]{2,0,1:T(8,128)S(1)} %maximum_convert_fusion, f32[3,2048]{1,0:T(4,128)S(1)} %get-tuple-element.14, f32[3,2048]{1,0:T(4,128)S(1)} %get-tuple-element.15, f32[3,2048]{1,0:T(4,128)S(1)} %get-tuple-element.16, f32[3,2048]{1,0:T(4,128)S(1)} %get-tuple-element.17, ...), kind=kLoop, calls=%fused_computation.16 | loop fusion | flops 15335424 | bytes 37920768 | tf_op jit(solution)/shard_map/add | solution.py:83
  21.0 54.8 %all-gather.2.cloned.1.call-done = bf16[192,8192]{1,0:T(8,128)(2,1)} async-done(((bf16[192,2048]{1,0:T(8,128)(2,1)}), bf16[192,8192]{1,0:T(8,128)(2,1)}) %all-gather.2.cloned.1.call-update) | async-done | bytes 3145744 | tf_op jit(solution)/shard_map/all_gather | solution.py:101
  75.7 18.5 %fusion.13 = (f32[192,2048]{1,0:T(8,128)S(1)}, f32[192,2048]{1,0:T(8,128)}) fusion(f32[192,3,2048]{2,0,1:T(8,128)} %fusion.7, bf16[192,8192]{1,0:T(8,128)(2,1)} %all-gather.2.cloned.1.call-done, bf16[2048,8192]{1,0:T(8,128)(2,1)} %param.8), kind=kOutput, calls=%fused_computation.39 | convolution fusion | flops 6442844160 | bytes 41418752 | tf_op jit(solution)/shard_map/te,ce->tc/dot_general | solution.py:102
  94.2 0.1 slice.126
  94.3 1.3 collective-permute-start.2
  95.6 0.7 pad.8.base_ref
  96.3 0.1 pad.21.clone
  96.4 2.5 collective-permute-done.2
  98.8 1.9 maximum_maximum_fusion.1.ext_ref
  100.7 20.2 %shard_map.69 = f32[192,2048]{1,0:T(8,128)} custom-call(f32[128,384]{1,0:T(8,128)} %pad.8.base_ref, f32[384,2048]{1,0:T(8,128)} %maximum_maximum_fusion.1.ext_ref), custom_call_target="tpu_custom_call" | custom-call | flops 7247757312 | bytes 4915200 | tf_op jit(solution)/shard_map/pallas_call | solution.py:41
  120.9 2.9 %multiply_bitcast_fusion.1 = (f32[192,1,2048]{2,0,1:T(8,128)S(1)}, f32[192,1,2048]{2,0,1:T(8,128)S(1)}, f32[192,2048]{1,0:T(8,128)S(1)}) fusion(f32[192,2048]{1,0:T(8,128)} %shard_map.69, f32[192,3,2048]{2,0,1:T(8,128)} %fusion.7), kind=kLoop, calls=%fused_computation.36 | loop fusion | flops 1179648 | bytes 9437184 | tf_op jit(solution)/shard_map/stack | solution.py:112
  123.8 1.2 copy-done
  125.0 1.1 slice.125
  126.1 14.3 %collective-permute-start.1 = (f32[127,2048]{1,0:T(8,128)}, f32[127,2048]{1,0:T(8,128)}, u32[]{:S(2)}, u32[]{:S(2)}) collective-permute-start(f32[127,2048]{1,0:T(8,128)} %slice.125), channel_id=1, source_target_pairs={{0,4},{4,8},{8,12},{12,16},{16,20},{20,24},{24,28},{1,5},{5,9},{9,... | collective-permute-start | bytes 3121160 | tf_op jit(solution)/shard_map/ppermute | solution.py:89
  140.4 0.1 rev.3
  140.5 0.7 pad.7.base_ref
  141.2 0.9 collective-permute-done.1
  142.1 3.6 %maximum_maximum_fusion.ext_ref = f32[384,2048]{1,0:T(8,128)} fusion(f32[192,2048]{1,0:T(8,128)} %copy-done, f32[127,2048]{1,0:T(8,128)} %collective-permute-done.1, f32[384]{0:T(512)S(1)} %pad.21.clone), kind=kLoop, calls=%fused_computation.29 | loop fusion | flops 1572864 | bytes 5760512 | tf_op jit(solution)/shard_map/concatenate | solution.py:90
  145.7 20.2 %shard_map.68 = f32[192,2048]{1,0:T(8,128)} custom-call(f32[128,384]{1,0:T(8,128)} %pad.7.base_ref, f32[384,2048]{1,0:T(8,128)} %maximum_maximum_fusion.ext_ref), custom_call_target="tpu_custom_call" | custom-call | flops 7247757312 | bytes 4915200 | tf_op jit(solution)/shard_map/pallas_call | solution.py:41
  165.9 16.7 %convolution_convert_fusion = bf16[192,8192]{1,0:T(8,128)(2,1)} fusion(bf16[2048,8192]{1,0:T(8,128)(2,1)} %param.8, f32[192,2048]{1,0:T(8,128)} %shard_map.68, f32[192,3,2048]{2,0,1:T(8,128)} %fusion.7), kind=kOutput, calls=%fused_computation | convolution fusion | flops 6444810240 | bytes 39845888 | tf_op jit(solution)/shard_map/tc,cd->td/dot_general | solution.py:96
  182.6 2.1 multiply_bitcast_fusion.2
  184.7 0.4 pad_maximum_fusion.1
  185.1 1.3 collective-permute-start.3
  186.4 11.0 %collective-permute-done.3 = f32[6,3,2048]{2,0,1:T(8,128)S(1)} collective-permute-done((f32[6,3,2048]{2,0,1:T(8,128)S(1)}, f32[6,3,2048]{2,0,1:T(8,128)S(1)}, u32[]{:S(2)}, u32[]{:S(2)}) %collective-permute-start.3) | collective-permute-done | bytes 147488 | tf_op jit(solution)/shard_map/ppermute | solution.py:113
  197.4 0.4 pad_maximum_fusion
  197.8 5.0 %fusion.1 = bf16[192,3,2048]{2,0,1:T(8,128)(2,1)} fusion(f32[198,3,2048]{2,0,1:T(8,128)S(1)} %pad_maximum_fusion, f32[3,2048]{1,0:T(4,128)S(1)} %get-tuple-element.14, f32[3,2048]{1,0:T(4,128)S(1)} %get-tuple-element.15, f32[3,2048]{1,0:T(4,128)S(1)} %get-tuple-element.16, f32[3,2048]{1,0:T(4,128)S(1)} %get-tuple-element.17, ...), kind=kLoop, calls=%fused_computation.4 | loop fusion | flops 18874368 | bytes 35561472 | tf_op jit(solution)/shard_map/convert_element_type | solution.py:118
  202.8 50.2 %reduce-scatter.2.cloned.1.call-done = bf16[192,2048]{1,0:T(8,128)(2,1)} async-done(((bf16[192,8192]{1,0:T(8,128)(2,1)}), bf16[192,2048]{1,0:T(8,128)(2,1)}) %reduce-scatter.2.cloned.1.call-update) | async-done | bytes 786448 | tf_op jit(solution)/shard_map/reduce_scatter | solution.py:99
  (13 shorter events, 0.2 us)
Async XLA Ops:
  7.2 68.6 %all-gather.2.cloned.1.call-start = ((), (), s32[]{:S(2)}) async-start(), calls=%async_computation.2 | async-start | bytes 3932160 | tf_op jit(solution)/shard_map/all_gather | solution.py:101
  7.9 245.1 %reduce-scatter.2.cloned.1.call-start = ((), (), s32[]{:S(2)}) async-start(), calls=%async_computation.1 | async-start | bytes 3932160 | tf_op jit(solution)/shard_map/reduce_scatter | solution.py:99
  8.9 4.4 %collective-permute-start = (bf16[6,3,2048]{2,0,1:T(8,128)(2,1)S(1)}, bf16[6,3,2048]{2,0,1:T(8,128)(2,1)S(1)}, u32[]{:S(2)}, u32[]{:S(2)}) collective-permute-start(bf16[6,3,2048]{2,0,1:T(8,128)(2,1)S(1)} %slice.89), channel_id=1, source_target_pairs={{0,4},{4,8},{8,12},{12,16},{16,20},{20,24},{24,28},{1,5},{5,9},{9,... | collective-permute-start | bytes 221192 | tf_op jit(solution)/shard_map/ppermute | solution.py:79
  21.0 74.6 %copy-start.1 = (f32[128,128]{1,0:T(8,128)S(1)}, f32[128,128]{1,0:T(8,128)}, u32[]{:S(2)}) copy-start(f32[128,128]{1,0:T(8,128)} %param.7) | copy-start | bytes 196612
  94.3 4.6 %collective-permute-start.2 = (f32[127,2048]{1,0:T(8,128)S(1)}, f32[127,2048]{1,0:T(8,128)S(1)}, u32[]{:S(2)}, u32[]{:S(2)}) collective-permute-start(f32[127,2048]{1,0:T(8,128)S(1)} %slice.126), channel_id=1, source_target_pairs={{4,0},{8,4},{12,8},{16,12},{20,16},{24,20},{28,24},{5,1},{9,5},{13... | collective-permute-start | bytes 3121160 | tf_op jit(solution)/shard_map/ppermute | solution.py:107
  123.8 1.2 copy-start
  126.1 15.9 %collective-permute-start.1 = (f32[127,2048]{1,0:T(8,128)}, f32[127,2048]{1,0:T(8,128)}, u32[]{:S(2)}, u32[]{:S(2)}) collective-permute-start(f32[127,2048]{1,0:T(8,128)} %slice.125), channel_id=1, source_target_pairs={{0,4},{4,8},{8,12},{12,16},{16,20},{20,24},{24,28},{1,5},{5,9},{9,... | collective-permute-start | bytes 3121160 | tf_op jit(solution)/shard_map/ppermute | solution.py:89
  185.1 12.3 %collective-permute-start.3 = (f32[6,3,2048]{2,0,1:T(8,128)S(1)}, f32[6,3,2048]{2,0,1:T(8,128)S(1)}, u32[]{:S(2)}, u32[]{:S(2)}) collective-permute-start(f32[6,3,2048]{2,0,1:T(8,128)S(1)} %slice.127), channel_id=1, source_target_pairs={{4,0},{8,4},{12,8},{16,12},{20,16},{24,20},{28,24},{5,1},{9,5},{13... | collective-permute-start | bytes 442376 | tf_op jit(solution)/shard_map/ppermute | solution.py:113
Sparse Core Ops, SparseCore 0:
  9.5 66.1 all-gather.1
  182.7 70.2 reduce-scatter.1
where the time goes:
time: 260 us
  waiting for transfers between devices  120 us (46%)
  Pallas kernels  40.4 us (16%)
  matrix products  35.1 us (14%)
  other arithmetic  24 us (9%)
  starting transfers between devices  19.4 us (7%)
  between operations  14.2 us (5%)
  local copies, waits for them, and re-layouts  6.81 us (3%)
    all_gather x1, waiting for transfers between devices, body(): cot_full = lax.all_gather(cotangent, 'tp', axis=1, tiled=True)  54.8 us
    reduce_scatter x1, waiting for transfers between devices, body(): output = lax.psum_scatter(partial, 'tp', scatter_dimension=1, tiled=True)  50.2 us
    pallas_call x2, Pallas kernels, toeplitz_conv(): pl.pallas_call(_toeplitz_kernel, grid=(steps,), in_specs=[pl.BlockSpec((g...  40.4 us
    dot_general x1, matrix products, body(): jnp.einsum('te,ce->tc', cot_full, out_weight, preferred_element_type=jnp....  18.5 us
    dot_general x1, matrix products, body(): jnp.einsum('tc,cd->td', mixed, out_weight, preferred_element_type=jnp.flo...  16.7 us
    ppermute x1, starting transfers between devices, body(): prev_prod = lax.ppermute(product[rows - lh:], 'seq', fwd)  14.3 us
    ppermute x1, waiting for transfers between devices, body(): next_dfeat = lax.ppermute(dfeat[:fh], 'seq', bwd)  11 us
    another operation x3, other arithmetic, body(): jnp.stack([query_grad, conv_grad * value_feat, conv_grad * key_feat], axi...  5.33 us
  transfers between devices with their start and end apart: 6, of which 5 were waited for; matrix products, arithmetic and copies ran while one was open for 8% of the time, Pallas kernels for 0%

commit v1 on v0

--- a/solution.py
+++ b/solution.py
@@ -59,7 +59,7 @@
     return [(j + 1, j) for j in range(n - 1)]
 
 
-def body(projected, feat_taps, filters, out_weight, cotangent):
+def block(projected, feat_taps, filters, out_weight, cotangent):
     rows = projected.shape[0]
     feat_len = feat_taps.shape[0]
     filt_len = filters.shape[1]
@@ -98,6 +98,9 @@
     ).astype(jnp.bfloat16)
     output = lax.psum_scatter(partial, "tp", scatter_dimension=1, tiled=True)
 
+    query, key_feat, value_feat, conv = lax.optimization_barrier(
+        (query, key_feat, value_feat, conv)
+    )
     cot_full = lax.all_gather(cotangent, "tp", axis=1, tiled=True)
     grad_mixed = jnp.einsum(
         "te,ce->tc", cot_full, out_weight, preferred_element_type=jnp.float32
@@ -127,4 +130,4 @@
         P("seq", "tp"),
     )
     out_specs = (P("seq", "tp"), P("seq", None, "tp"))
-    return jax.shard_map(body, mesh=mesh, in_specs=in_specs, out_specs=out_specs, check_vma=False)
+    return jax.shard_map(block, mesh=mesh, in_specs=in_specs, out_specs=out_specs, check_vma=False)

time: 260 us -> 164 us (0.63)
  the two profiles are of different devices: /device:TPU:0 before, /device:TPU:27 now
where the time goes in v1:
time: 164 us
  Pallas kernels  40.3 us (25%)
  matrix products  34.7 us (21%)
  waiting for transfers between devices  27.5 us (17%)
  other arithmetic  21.7 us (13%)
  between operations  14.2 us (9%)
  starting transfers between devices  13 us (8%)
  local copies, waits for them, and re-layouts  12.3 us (8%)
    pallas_call x2, Pallas kernels, toeplitz_conv(): pl.pallas_call(_toeplitz_kernel, grid=(steps,), in_specs=[pl.BlockSpec((g...  40.3 us
    dot_general x1, matrix products, block(): jnp.einsum('te,ce->tc', cot_full, out_weight, preferred_element_type=jnp....  18 us
    dot_general x1, matrix products, block(): jnp.einsum('tc,cd->td', mixed, out_weight, preferred_element_type=jnp.flo...  16.7 us
    ppermute x1, waiting for transfers between devices, block(): next_sig = lax.ppermute(signal_grad[:lh], 'seq', bwd)  14.9 us
    ppermute x1, waiting for transfers between devices, block(): prev_prod = lax.ppermute(product[rows - lh:], 'seq', fwd)  6.58 us
    ppermute x1, waiting for transfers between devices, block(): next_dfeat = lax.ppermute(dfeat[:fh], 'seq', bwd)  5.96 us
    convert_element_type x1, other arithmetic, block(): return (output, igrad.astype(jnp.bfloat16))  4.99 us
    ppermute x1, starting transfers between devices, block(): prev_prod = lax.ppermute(product[rows - lh:], 'seq', fwd)  4.76 us
  transfers between devices with their start and end apart: 6, of which 3 were waited for; matrix products, arithmetic and copies ran while one was open for 40% of the time, Pallas kernels for 25%

profile of v1, /device:TPU:27, one launch (start us, length us, event | category | flops | bytes accessed | tf_op | source)
XLA Modules:
  0.0 163.8 jit_solution(1891076096759250459)
XLA Ops:
  7.2 0.9 slice.89
  8.1 3.7 %collective-permute-start = (bf16[6,3,2048]{2,0,1:T(8,128)(2,1)S(1)}, bf16[6,3,2048]{2,0,1:T(8,128)(2,1)S(1)}, u32[]{:S(2)}, u32[]{:S(2)}) collective-permute-start(bf16[6,3,2048]{2,0,1:T(8,128)(2,1)S(1)} %slice.89), channel_id=1, source_target_pairs={{0,4},{4,8},{8,12},{12,16},{16,20},{20,24},{24,28},{1,5},{5,9},{9,... | collective-permute-start | bytes 221192 | tf_op jit(solution)/shard_map/ppermute | solution.py:79
  11.8 0.0 reduce-scatter.2.cloned.1.call-start
  11.9 1.8 %fusion.14 = (f32[1,3,2048]{2,0,1:T(1,128)S(1)}, f32[1,3,2048]{2,0,1:T(1,128)S(1)}, f32[1,3,2048]{2,0,1:T(1,128)S(1)}, f32[1,3,2048]{2,0,1:T(1,128)S(1)}, f32[1,...) fusion(f32[7,3,2048]{2,0,1:T(8,128)} %param.6), kind=kLoop, calls=%fused_computation.47 | loop fusion | bytes 344064 | tf_op jit(solution)/shard_map/slice | solution.py:81
  13.9 2.4 %maximum_convert_fusion = f32[198,3,2048]{2,0,1:T(8,128)S(1)} fusion(bf16[192,3,2048]{2,0,1:T(8,128)(2,1)} %param.5, bf16[6,3,2048]{2,0,1:T(8,128)(2,1)S(1)} %collective-permute-done), kind=kLoop, calls=%fused_computation.31 | loop fusion | flops 4866048 | bytes 7299072 | tf_op jit(solution)/shard_map/convert_element_type | solution.py:80
  16.3 3.9 %fusion.7 = f32[192,3,2048]{2,0,1:T(8,128)S(1)} fusion(f32[198,3,2048]{2,0,1:T(8,128)S(1)} %maximum_convert_fusion, f32[3,2048]{1,0:T(4,128)S(1)} %get-tuple-element.24, f32[3,2048]{1,0:T(4,128)S(1)} %get-tuple-element.25, f32[3,2048]{1,0:T(4,128)S(1)} %get-tuple-element.26, f32[3,2048]{1,0:T(4,128)S(1)} %get-tuple-element.27, ...), kind=kLoop, calls=%fused_computation.16 | loop fusion | flops 15335424 | bytes 37920768 | tf_op jit(solution)/shard_map/add | solution.py:83
  20.2 2.1 %copy-done = f32[192,3,2048]{2,0,1:T(8,128)} copy-done((f32[192,3,2048]{2,0,1:T(8,128)}, f32[192,3,2048]{2,0,1:T(8,128)S(1)}, u32[]{:S(2)}) %copy-start) | copy-done | bytes 4718616
  22.3 0.2 fusion.13
  22.4 1.1 slice.125
  23.5 4.8 %collective-permute-start.1 = (f32[127,2048]{1,0:T(8,128)}, f32[127,2048]{1,0:T(8,128)}, u32[]{:S(2)}, u32[]{:S(2)}) collective-permute-start(f32[127,2048]{1,0:T(8,128)} %slice.125), channel_id=1, source_target_pairs={{0,4},{4,8},{8,12},{12,16},{16,20},{20,24},{24,28},{1,5},{5,9},{9,... | collective-permute-start | bytes 3121160 | tf_op jit(solution)/shard_map/ppermute | solution.py:89
  28.3 0.1 rev.3
  28.4 0.7 pad.7.base_ref
  29.1 0.1 pad.21.clone
  29.1 4.6 %slice_bitcast_fusion = (f32[192,2048]{1,0:T(8,128)S(1)}, f32[192,2048]{1,0:T(8,128)}, f32[192,2048]{1,0:T(8,128)}) fusion(f32[192,3,2048]{2,0,1:T(8,128)} %copy-done), kind=kLoop, calls=%fused_computation.32 | loop fusion | bytes 9437184 | tf_op jit(solution)/shard_map/squeeze | solution.py:86
  33.7 6.6 %collective-permute-done.1 = f32[127,2048]{1,0:T(8,128)} collective-permute-done((f32[127,2048]{1,0:T(8,128)}, f32[127,2048]{1,0:T(8,128)}, u32[]{:S(2)}, u32[]{:S(2)}) %collective-permute-start.1) | collective-permute-done | bytes 1040416 | tf_op jit(solution)/shard_map/ppermute | solution.py:89
  40.3 3.3 %maximum_maximum_fusion.ext_ref = f32[384,2048]{1,0:T(8,128)} fusion(f32[192,2048]{1,0:T(8,128)S(1)} %fusion.13, f32[127,2048]{1,0:T(8,128)} %collective-permute-done.1, f32[384]{0:T(512)S(1)} %pad.21.clone), kind=kLoop, calls=%fused_computation.29 | loop fusion | flops 1572864 | bytes 5760512 | tf_op jit(solution)/shard_map/concatenate | solution.py:90
  43.6 20.2 %shard_map.68 = f32[192,2048]{1,0:T(8,128)} custom-call(f32[128,384]{1,0:T(8,128)} %pad.7.base_ref, f32[384,2048]{1,0:T(8,128)} %maximum_maximum_fusion.ext_ref), custom_call_target="tpu_custom_call" | custom-call | flops 7247757312 | bytes 4915200 | tf_op jit(solution)/shard_map/pallas_call | solution.py:41
  63.8 16.7 %convolution_convert_fusion = bf16[192,8192]{1,0:T(8,128)(2,1)} fusion(bf16[2048,8192]{1,0:T(8,128)(2,1)} %param.8, f32[192,2048]{1,0:T(8,128)} %shard_map.68, f32[192,3,2048]{2,0,1:T(8,128)} %copy-done), kind=kOutput, calls=%fused_computation | convolution fusion | flops 6444810240 | bytes 39845888 | tf_op jit(solution)/shard_map/tc,cd->td/dot_general | solution.py:96
  80.5 18.0 %fusion.15 = f32[192,2048]{1,0:T(8,128)} fusion(bf16[192,8192]{1,0:T(8,128)(2,1)} %all-gather.2.cloned.1.call-done, bf16[2048,8192]{1,0:T(8,128)(2,1)} %param.8), kind=kOutput, calls=%fused_computation.48 | convolution fusion | flops 6442450944 | bytes 38273024 | tf_op jit(solution)/shard_map/te,ce->tc/dot_general | solution.py:105
  98.6 1.8 %multiply_bitcast_fusion.2 = (f32[192,1,2048]{2,0,1:T(8,128)S(1)}, f32[192,2048]{1,0:T(8,128)S(1)}) fusion(f32[192,2048]{1,0:T(8,128)} %fusion.15, f32[192,2048]{1,0:T(8,128)S(1)} %copy-done.2, f32[192,2048]{1,0:T(8,128)S(1)} %copy-done.1), kind=kLoop, calls=%fused_computation.37 | loop fusion | flops 786432 | bytes 7864320 | tf_op jit(solution)/shard_map/stack | solution.py:115
  100.4 0.1 slice.126
  100.4 2.6 %collective-permute-start.2 = (f32[127,2048]{1,0:T(8,128)S(1)}, f32[127,2048]{1,0:T(8,128)S(1)}, u32[]{:S(2)}, u32[]{:S(2)}) collective-permute-start(f32[127,2048]{1,0:T(8,128)S(1)} %slice.126), channel_id=1, source_target_pairs={{4,0},{8,4},{12,8},{16,12},{20,16},{24,20},{28,24},{5,1},{9,5},{13... | collective-permute-start | bytes 3121160 | tf_op jit(solution)/shard_map/ppermute | solution.py:110
  103.0 0.7 pad.8.base_ref
  103.7 14.9 %collective-permute-done.2 = f32[127,2048]{1,0:T(8,128)S(1)} collective-permute-done((f32[127,2048]{1,0:T(8,128)S(1)}, f32[127,2048]{1,0:T(8,128)S(1)}, u32[]{:S(2)}, u32[]{:S(2)}) %collective-permute-start.2) | collective-permute-done | bytes 1040416 | tf_op jit(solution)/shard_map/ppermute | solution.py:110
  118.6 1.9 %maximum_maximum_fusion.1.ext_ref = f32[384,2048]{1,0:T(8,128)} fusion(f32[127,2048]{1,0:T(8,128)S(1)} %collective-permute-done.2, f32[192,2048]{1,0:T(8,128)S(1)} %get-tuple-element.14, f32[384]{0:T(512)S(1)} %pad.21.clone), kind=kLoop, calls=%fused_computation.30 | loop fusion | flops 1572864 | bytes 5760512 | tf_op jit(solution)/shard_map/concatenate | solution.py:111
  120.5 20.2 %shard_map.69 = f32[192,2048]{1,0:T(8,128)} custom-call(f32[128,384]{1,0:T(8,128)} %pad.8.base_ref, f32[384,2048]{1,0:T(8,128)} %maximum_maximum_fusion.1.ext_ref), custom_call_target="tpu_custom_call" | custom-call | flops 7247757312 | bytes 4915200 | tf_op jit(solution)/shard_map/pallas_call | solution.py:41
  140.7 2.3 %multiply_bitcast_fusion.1 = (f32[192,1,2048]{2,0,1:T(8,128)S(1)}, f32[192,1,2048]{2,0,1:T(8,128)S(1)}) fusion(f32[192,2048]{1,0:T(8,128)} %shard_map.69, f32[192,2048]{1,0:T(8,128)S(1)} %get-tuple-element.8, f32[192,2048]{1,0:T(8,128)} %get-tuple-element.9), kind=kLoop, calls=%fused_computation.36 | loop fusion | flops 786432 | bytes 7864320 | tf_op jit(solution)/shard_map/stack | solution.py:115
  143.0 0.5 pad_maximum_fusion.1
  143.5 1.9 %collective-permute-start.3 = (f32[6,3,2048]{2,0,1:T(8,128)S(1)}, f32[6,3,2048]{2,0,1:T(8,128)S(1)}, u32[]{:S(2)}, u32[]{:S(2)}) collective-permute-start(f32[6,3,2048]{2,0,1:T(8,128)S(1)} %slice.127), channel_id=1, source_target_pairs={{4,0},{8,4},{12,8},{16,12},{20,16},{24,20},{28,24},{5,1},{9,5},{13... | collective-permute-start | bytes 442376 | tf_op jit(solution)/shard_map/ppermute | solution.py:116
  145.5 6.0 %collective-permute-done.3 = f32[6,3,2048]{2,0,1:T(8,128)S(1)} collective-permute-done((f32[6,3,2048]{2,0,1:T(8,128)S(1)}, f32[6,3,2048]{2,0,1:T(8,128)S(1)}, u32[]{:S(2)}, u32[]{:S(2)}) %collective-permute-start.3) | collective-permute-done | bytes 147488 | tf_op jit(solution)/shard_map/ppermute | solution.py:116
  151.4 0.5 pad_maximum_fusion
  151.9 5.0 %fusion.1 = bf16[192,3,2048]{2,0,1:T(8,128)(2,1)} fusion(f32[198,3,2048]{2,0,1:T(8,128)S(1)} %pad_maximum_fusion, f32[3,2048]{1,0:T(4,128)S(1)} %get-tuple-element.24, f32[3,2048]{1,0:T(4,128)S(1)} %get-tuple-element.25, f32[3,2048]{1,0:T(4,128)S(1)} %get-tuple-element.26, f32[3,2048]{1,0:T(4,128)S(1)} %get-tuple-element.27, ...), kind=kLoop, calls=%fused_computation.4 | loop fusion | flops 18874368 | bytes 35561472 | tf_op jit(solution)/shard_map/convert_element_type | solution.py:121
  (19 shorter events, 0.2 us)
Async XLA Ops:
  7.2 73.3 %all-gather.2.cloned.1.call-start = ((), (), s32[]{:S(2)}) async-start(), calls=%async_computation.2 | async-start | bytes 3932160 | tf_op jit(solution)/shard_map/all_gather | solution.py:104
  8.1 5.7 %collective-permute-start = (bf16[6,3,2048]{2,0,1:T(8,128)(2,1)S(1)}, bf16[6,3,2048]{2,0,1:T(8,128)(2,1)S(1)}, u32[]{:S(2)}, u32[]{:S(2)}) collective-permute-start(bf16[6,3,2048]{2,0,1:T(8,128)(2,1)S(1)} %slice.89), channel_id=1, source_target_pairs={{0,4},{4,8},{8,12},{12,16},{16,20},{20,24},{24,28},{1,5},{5,9},{9,... | collective-permute-start | bytes 221192 | tf_op jit(solution)/shard_map/ppermute | solution.py:79
  11.8 145.1 %reduce-scatter.2.cloned.1.call-start = ((), (), s32[]{:S(2)}) async-start(), calls=%async_computation.1 | async-start | bytes 3932160 | tf_op jit(solution)/shard_map/reduce_scatter | solution.py:99
  20.1 2.1 %copy-start = (f32[192,3,2048]{2,0,1:T(8,128)}, f32[192,3,2048]{2,0,1:T(8,128)S(1)}, u32[]{:S(2)}) copy-start(f32[192,3,2048]{2,0,1:T(8,128)S(1)} %fusion.7) | copy-start | bytes 14155780
  22.3 6.0 %copy-start.3 = (f32[128,128]{1,0:T(8,128)S(1)}, f32[128,128]{1,0:T(8,128)}, u32[]{:S(2)}) copy-start(f32[128,128]{1,0:T(8,128)} %param.7) | copy-start | bytes 196612
  23.5 16.8 %collective-permute-start.1 = (f32[127,2048]{1,0:T(8,128)}, f32[127,2048]{1,0:T(8,128)}, u32[]{:S(2)}, u32[]{:S(2)}) collective-permute-start(f32[127,2048]{1,0:T(8,128)} %slice.125), channel_id=1, source_target_pairs={{0,4},{4,8},{8,12},{12,16},{16,20},{20,24},{24,28},{1,5},{5,9},{9,... | collective-permute-start | bytes 3121160 | tf_op jit(solution)/shard_map/ppermute | solution.py:89
  80.5 18.1 %copy-start.1 = (f32[192,2048]{1,0:T(8,128)S(1)}, f32[192,2048]{1,0:T(8,128)}, u32[]{:S(2)}) copy-start(f32[192,2048]{1,0:T(8,128)} %get-tuple-element.7) | copy-start | bytes 4718596
  80.5 18.1 %copy-start.2 = (f32[192,2048]{1,0:T(8,128)S(1)}, f32[192,2048]{1,0:T(8,128)}, u32[]{:S(2)}) copy-start(f32[192,2048]{1,0:T(8,128)} %shard_map.68) | copy-start | bytes 4718596
  100.4 18.2 %collective-permute-start.2 = (f32[127,2048]{1,0:T(8,128)S(1)}, f32[127,2048]{1,0:T(8,128)S(1)}, u32[]{:S(2)}, u32[]{:S(2)}) collective-permute-start(f32[127,2048]{1,0:T(8,128)S(1)} %slice.126), channel_id=1, source_target_pairs={{4,0},{8,4},{12,8},{16,12},{20,16},{24,20},{28,24},{5,1},{9,5},{13... | collective-permute-start | bytes 3121160 | tf_op jit(solution)/shard_map/ppermute | solution.py:110
  143.5 7.9 %collective-permute-start.3 = (f32[6,3,2048]{2,0,1:T(8,128)S(1)}, f32[6,3,2048]{2,0,1:T(8,128)S(1)}, u32[]{:S(2)}, u32[]{:S(2)}) collective-permute-start(f32[6,3,2048]{2,0,1:T(8,128)S(1)} %slice.127), channel_id=1, source_target_pairs={{4,0},{8,4},{12,8},{16,12},{20,16},{24,20},{28,24},{5,1},{9,5},{13... | collective-permute-start | bytes 442376 | tf_op jit(solution)/shard_map/ppermute | solution.py:116
Sparse Core Ops, SparseCore 0:
  12.0 60.7 all-gather.1
  80.6 60.8 reduce-scatter.1
